TPU v7x, 128 devices: a whole 4x4x4 slice. The times are simulated.
128 devices in a mesh: ctx: 16 (over y, x), grp: 8 (over z, core).
Axes of the slice: x: 4, y: 4, z: 4, core: 2. Of those that a mesh axis runs over, the one named last changes fastest.
Arguments:
- residual: bfloat16 [8, 2048, 2880], P('grp', 'ctx'), may hold values from -3 to 3
- queries: bfloat16 [8, 2048, 2048], P('grp', 'ctx'), may hold values from -8 to 8
- stretch_kv: bfloat16 [8, 2048, 1024], P('grp', 'ctx'), may hold values from -8 to 8
- cache_kv: bfloat16 [8, 4096, 1024], P('grp', 'ctx'), may hold values from -6 to 6
- doc_lengths: int32 [8, 8], P('grp'), may hold values from 1 to 3072, 6144 in all within a row
- sinks: float32 [32], replicated, may hold values from 2 to 6
- out_proj: bfloat16 [2048, 2880], P('ctx'), may hold values from -0.75 to 0.75
- norm_gain: float32 [2880], replicated, may hold values from 0.1 to 1.9
- router: bfloat16 [2880, 64], replicated, may hold values from -0.109375 to 0.109375
- expert_ids: int32 [8, 2048, 4], P('grp', 'ctx'), may hold values from 0 to 63, all different within a row; in each aligned block of 128 rows (0 to 127, 128 to 255, ..., all dimensions but the last counted through in order) at most 10 rows name the same one
- expert_in: bfloat16 [128, 2880, 1536], P(('ctx', 'grp')), may hold values from -0.109375 to 0.109375
- expert_out: bfloat16 [128, 768, 2880], P(('ctx', 'grp')), may hold values from -0.15625 to 0.15625
Outputs:
- resid_mid: bfloat16 [8, 2048, 2880], P('grp', 'ctx')
- layer_out: bfloat16 [8, 2048, 2880], P('grp', 'ctx')
Inputs may be any that keep to these rules, and one draw needn't show every extreme that they name: `expert_ids`: in the rows of one device (aligned blocks of 128 tokens, sequence after sequence), each expert is named by at most 10 rows, and in some blocks one expert by exactly 10; a token's 4 experts differ. `doc_lengths`: A sequence's 8 lengths sum to 6144; the longest is exactly 3072.
All inputs are finite; a program needn't handle non-finite values.
Results may differ from a plain program's by a relative error of at most 0.015.
Values may be sent and summed in bfloat16 or wider, within the bound.
No kernel may reach another device: no remote copies, remote signals or barrier semaphores. Data moves between devices by JAX's collectives and lax.ppermute only.
A program may use at most 128 MiB of HBM per device.

v0:
```python
import math
import jax
import jax.numpy as jnp
from jax import lax
from jax.sharding import PartitionSpec as P

HEADS = 32
KVH = 8
HD = 64


def doc_index(positions, lengths):
    ends = jnp.cumsum(lengths)
    return jnp.sum((positions[:, None] >= ends[None, :]).astype(jnp.int32), axis=1)


def gated_act(pre, half_width):
    gate = pre[:, :half_width]
    upper = pre[:, half_width:]
    return ((upper + 1.0) * gate * jax.nn.sigmoid(1.702 * gate)).astype(jnp.bfloat16)


def body(
    residual,
    queries,
    stretch_kv,
    cache_kv,
    doc_lengths,
    sinks,
    out_proj,
    norm_gain,
    router,
    expert_ids,
    expert_in,
    expert_out,
):
    tokens = residual.shape[1]
    width = residual.shape[2]
    cache_rows = cache_kv.shape[1]
    kv_cols = stretch_kv.shape[2] // 2
    groups = HEADS // KVH
    ctx_count = lax.axis_size("ctx")
    ctx_here = lax.axis_index("ctx")
    stretch_base = cache_rows * ctx_count
    span = cache_rows + tokens
    query_pos = stretch_base + ctx_here * tokens + jnp.arange(tokens, dtype=jnp.int32)
    lengths = doc_lengths[0]
    query_doc = doc_index(query_pos, lengths)
    query_heads = queries[0].reshape(tokens, KVH, groups, HD)
    sink_grid = sinks.reshape(KVH, groups)
    local_kv = jnp.concatenate([cache_kv[0], stretch_kv[0]], axis=0)
    scale = 1.0 / math.sqrt(HD)

    def key_block(carry, keys_values, first):
        count = keys_values.shape[0]
        rows = first + jnp.arange(count, dtype=jnp.int32)
        source = rows // span
        offset = rows % span
        key_pos = jnp.where(
            offset < cache_rows,
            source * cache_rows + offset,
            stretch_base + source * tokens + offset - cache_rows,
        )
        key_doc = doc_index(key_pos, lengths)
        allowed = (key_pos[None, :] <= query_pos[:, None]) & (
            key_doc[None, :] == query_doc[:, None]
        )
        keys = keys_values[:, :kv_cols].reshape(count, KVH, HD)
        values = keys_values[:, kv_cols:].reshape(count, KVH, HD)
        top, total, numer = carry
        scores = (
            jnp.einsum("qkgd,skd->kgqs", query_heads, keys, preferred_element_type=jnp.float32)
            * scale
        )
        masked = jnp.where(allowed[None, None], scores, -jnp.inf)
        new_top = jnp.maximum(top, jnp.max(masked, axis=-1))
        weights = jnp.where(allowed[None, None], jnp.exp(scores - new_top[..., None]), 0.0)
        shrink = jnp.exp(top - new_top)
        total = total * shrink + jnp.sum(weights, axis=-1)
        numer = numer * shrink[..., None] + jnp.einsum(
            "kgqs,skd->kgqd",
            weights.astype(jnp.bfloat16),
            values,
            preferred_element_type=jnp.float32,
        )
        return (new_top, total, numer)

    start_top = jnp.broadcast_to(sink_grid[:, :, None], (KVH, groups, tokens))
    start_total = jnp.zeros((KVH, groups, tokens), jnp.float32)
    start_numer = jnp.zeros((KVH, groups, tokens, HD), jnp.float32)
    piece = lax.all_gather(local_kv, "ctx", axis=0, tiled=True)
    count = piece.shape[0]
    step_rows = math.gcd(count, 1024)

    def advance(index, state):
        first = index * step_rows
        part = lax.dynamic_slice_in_dim(piece, first, step_rows, 0)
        return key_block(state, part, first)

    top, total, numer = lax.fori_loop(
        0, count // step_rows, advance, (start_top, start_total, start_numer)
    )
    denom = total + jnp.exp(sink_grid[:, :, None] - top)
    attended = (
        jnp.transpose(numer / denom[..., None], (2, 0, 1, 3))
        .reshape(tokens, HEADS * HD)
        .astype(jnp.bfloat16)
    )
    grp_here = lax.axis_index("grp")
    parity = grp_here % 2
    grp_count = lax.axis_size("grp")
    pair_perm = [(g, g ^ 1) for g in range(grp_count)]
    head_rows = out_proj.shape[0] // 2
    proj_half = lax.all_gather(
        lax.dynamic_slice_in_dim(out_proj, parity * head_rows, head_rows, 0),
        "ctx",
        axis=0,
        tiled=True,
    )
    by_parity = attended.reshape(tokens, HEADS // 2, 2, HD)
    mine = jnp.where(parity == 0, by_parity[:, :, 0], by_parity[:, :, 1]).reshape(tokens, -1)
    theirs_cols = jnp.where(parity == 0, by_parity[:, :, 1], by_parity[:, :, 0]).reshape(tokens, -1)
    partner_cols = lax.ppermute(theirs_cols, "grp", pair_perm)
    both = jnp.dot(
        jnp.concatenate([mine, partner_cols], axis=0), proj_half, preferred_element_type=jnp.float32
    )
    back = lax.ppermute(both[tokens:], "grp", pair_perm)
    projected = both[:tokens] + back
    mid = (residual[0].astype(jnp.float32) + projected).astype(jnp.bfloat16)
    mid_float = mid.astype(jnp.float32)
    normed = (
        mid_float
        * lax.rsqrt(jnp.mean(mid_float * mid_float, axis=-1, keepdims=True) + 1e-05)
        * norm_gain
    ).astype(jnp.bfloat16)
    logits = jnp.dot(normed, router, preferred_element_type=jnp.float32)
    experts = router.shape[1]
    chosen_ids = expert_ids[0]
    topk = chosen_ids.shape[1]
    picks = chosen_ids[:, :, None] == jnp.arange(experts, dtype=jnp.int32)[None, None, :]
    chosen = jnp.sum(jnp.where(picks, logits[:, None, :], 0.0), axis=-1)
    raised = jnp.exp(chosen)
    route_weights = raised / jnp.sum(raised, axis=-1, keepdims=True)
    capacity = 2 * ((5 * tokens * topk + 8 * experts - 1) // (8 * experts))
    flat_ids = chosen_ids.reshape(-1)
    pairs = flat_ids.shape[0]
    onehot = (flat_ids[:, None] == jnp.arange(experts, dtype=jnp.int32)[None, :]).astype(jnp.int32)
    slots = jnp.sum(onehot * (jnp.cumsum(onehot, axis=0) - 1), axis=1)
    dest = flat_ids * capacity + slots
    source_rows = jnp.arange(pairs, dtype=jnp.int32) // topk
    packed = jnp.zeros((experts * capacity, width), jnp.bfloat16).at[dest].set(normed[source_rows])
    packed = packed.reshape(experts, capacity, width)
    in_weights = expert_in[0]
    out_weights = expert_out[0]
    half_width = out_weights.shape[0]
    owners = 2 * experts
    half_cap = capacity // 2
    split = packed.reshape(owners, half_cap, width)
    received = lax.all_to_all(split, ("ctx", "grp"), split_axis=0, concat_axis=0, tiled=True)
    partner_rows = lax.ppermute(received, "grp", pair_perm)

    def expert_half(rows):
        pre = jnp.dot(rows.reshape(-1, width), in_weights, preferred_element_type=jnp.float32)
        hidden = gated_act(pre, half_width)
        return jnp.dot(hidden, out_weights, preferred_element_type=jnp.float32).astype(jnp.bfloat16)

    own_part = expert_half(received)
    partner_part = expert_half(partner_rows)
    partner_back = lax.ppermute(partner_part, "grp", pair_perm)
    summed = (own_part.astype(jnp.float32) + partner_back.astype(jnp.float32)).astype(jnp.bfloat16)
    returned = lax.all_to_all(
        summed.reshape(owners, half_cap, width),
        ("ctx", "grp"),
        split_axis=0,
        concat_axis=0,
        tiled=True,
    )
    expert_rows = returned.reshape(experts * capacity, width)
    gathered = expert_rows[dest].astype(jnp.float32) * route_weights.reshape(-1)[:, None]
    mixture = jnp.sum(gathered.reshape(tokens, topk, width), axis=1)
    final = (mid_float + mixture).astype(jnp.bfloat16)
    return (mid[None], final[None])


def solution(mesh):
    return jax.shard_map(
        body,
        mesh=mesh,
        in_specs=(
            P("grp", "ctx", None),
            P("grp", "ctx", None),
            P("grp", "ctx", None),
            P("grp", "ctx", None),
            P("grp", None),
            P(),
            P("ctx", None),
            P(),
            P(),
            P("grp", "ctx", None),
            P(("ctx", "grp"), None, None),
            P(("ctx", "grp"), None, None),
        ),
        out_specs=(P("grp", "ctx", None), P("grp", "ctx", None)),
        check_vma=False,
    )
```

profile of v0, /device:TPU:1, one launch (start us, length us, event | category | flops | bytes accessed | tf_op | source)
XLA Modules:
  0.0 601.9 jit_solution(10687653311530739906)
XLA Ops:
  12.9 99.8 %all-gather.3.cloned.1.call-done = bf16[6144,1024]{0,1:T(8,128)(2,1)} async-done(((bf16[384,1024]{0,1:T(8,128)(2,1)}), bf16[6144,1024]{0,1:T(8,128)(2,1)}) %all-gather.3.cloned.1.call-update) | async-done | bytes 12582928 | tf_op jit(solution)/shard_map/all_gather | solution.py:91
  112.8 156.1 %while.20 = (s32[]{:T(128)}, f32[8,4,128]{2,1,0:T(4,128)S(1)}, f32[8,4,128]{2,1,0:T(4,128)S(1)}, f32[8,4,128,64]{2,3,1,0:T(8,128)S(1)}, s32[1,8]{1,0:T(1,128)S(1...) while((s32[]{:T(128)}, f32[8,4,128]{2,1,0:T(4,128)S(1)}, ...), condition=%wide.region_7.8_spmd.clone, body=%wide.region_3.7_spmd.clone.sunk | while | flops 1121116288 | bytes 60053240 | solution.py:100
  115.0 7.1 %fusion.89 = (f32[8,4,128]{2,1,0:T(4,128)S(1)}, f32[8,1024,128,4]{2,1,3,0:T(8,128)}) fusion(pred[128,1024]{0,1:T(8,128)(4,1)S(1)} %compare_and_fusion.2, bf16[1024,8,64,1]{0,2,3,1:T(8,128)(2,1)S(1)} %bitcast.101, bf16[128,8,4,64]{0,3,2,1:T(8,128)(2,1)S(1)} %get-tuple-element.396), kind=kOutput, calls=%fused_computation.6.clone.1 | convolution fusion | flops 549449728 | bytes 18497536 | tf_op jit(solution)/shard_map/while/body/eval_jaxpr/qkgd,skd->kgqs/dot_general | solution.py:72
  122.0 9.5 %fusion.90 = f32[8,4,128]{2,1,0:T(4,128)S(1)} fusion(f32[8,1024,128,4]{2,1,3,0:T(8,128)} %get-tuple-element.357, f32[8,4,128]{2,1,0:T(4,128)S(1)} %max.12, pred[128,1024]{0,1:T(8,128)(4,1)S(1)} %compare_and_fusion.2), kind=kLoop, calls=%fused_computation.10.clone.1 | loop fusion | flops 16773120 | bytes 16941056 | tf_op jit(solution)/shard_map/while/body/eval_jaxpr/reduce_sum | solution.py:79
  131.6 7.6 %fusion.92 = f32[8,4,128,64]{2,3,1,0:T(8,128)S(1)} fusion(bf16[1024,8,64,1]{0,2,3,1:T(8,128)(2,1)S(1)} %bitcast.103, f32[8,1024,128,4]{2,1,3,0:T(8,128)} %get-tuple-element.357, f32[8,4,128]{2,1,0:T(4,128)S(1)} %max.12, pred[128,1024]{0,1:T(8,128)(4,1)S(1)} %compare_and_fusion.2, f32[8,4,128,64]{2,3,1,0:T(8,128)S(1)} %get-tuple-element.378, ...), kind=kOutput, calls=%fused_computation.13.clone.1 | convolution fusion | flops 554434560 | bytes 20086784 | tf_op jit(solution)/shard_map/while/body/eval_jaxpr/kgqs,skd->kgqd/dot_general | solution.py:80
  141.4 7.3 %fusion.89 = (f32[8,4,128]{2,1,0:T(4,128)S(1)}, f32[8,1024,128,4]{2,1,3,0:T(8,128)}) fusion(pred[128,1024]{0,1:T(8,128)(4,1)S(1)} %compare_and_fusion.2, bf16[1024,8,64,1]{0,2,3,1:T(8,128)(2,1)S(1)} %bitcast.101, bf16[128,8,4,64]{0,3,2,1:T(8,128)(2,1)S(1)} %get-tuple-element.396), kind=kOutput, calls=%fused_computation.6.clone.1 | convolution fusion | flops 549449728 | bytes 18497536 | tf_op jit(solution)/shard_map/while/body/eval_jaxpr/qkgd,skd->kgqs/dot_general | solution.py:72
  148.7 9.1 %fusion.90 = f32[8,4,128]{2,1,0:T(4,128)S(1)} fusion(f32[8,1024,128,4]{2,1,3,0:T(8,128)} %get-tuple-element.357, f32[8,4,128]{2,1,0:T(4,128)S(1)} %max.12, pred[128,1024]{0,1:T(8,128)(4,1)S(1)} %compare_and_fusion.2), kind=kLoop, calls=%fused_computation.10.clone.1 | loop fusion | flops 16773120 | bytes 16941056 | tf_op jit(solution)/shard_map/while/body/eval_jaxpr/reduce_sum | solution.py:79
  157.8 7.7 %fusion.92 = f32[8,4,128,64]{2,3,1,0:T(8,128)S(1)} fusion(bf16[1024,8,64,1]{0,2,3,1:T(8,128)(2,1)S(1)} %bitcast.103, f32[8,1024,128,4]{2,1,3,0:T(8,128)} %get-tuple-element.357, f32[8,4,128]{2,1,0:T(4,128)S(1)} %max.12, pred[128,1024]{0,1:T(8,128)(4,1)S(1)} %compare_and_fusion.2, f32[8,4,128,64]{2,3,1,0:T(8,128)S(1)} %get-tuple-element.378, ...), kind=kOutput, calls=%fused_computation.13.clone.1 | convolution fusion | flops 554434560 | bytes 20086784 | tf_op jit(solution)/shard_map/while/body/eval_jaxpr/kgqs,skd->kgqd/dot_general | solution.py:80
  167.9 7.0 %fusion.89 = (f32[8,4,128]{2,1,0:T(4,128)S(1)}, f32[8,1024,128,4]{2,1,3,0:T(8,128)}) fusion(pred[128,1024]{0,1:T(8,128)(4,1)S(1)} %compare_and_fusion.2, bf16[1024,8,64,1]{0,2,3,1:T(8,128)(2,1)S(1)} %bitcast.101, bf16[128,8,4,64]{0,3,2,1:T(8,128)(2,1)S(1)} %get-tuple-element.396), kind=kOutput, calls=%fused_computation.6.clone.1 | convolution fusion | flops 549449728 | bytes 18497536 | tf_op jit(solution)/shard_map/while/body/eval_jaxpr/qkgd,skd->kgqs/dot_general | solution.py:72
  174.9 9.1 %fusion.90 = f32[8,4,128]{2,1,0:T(4,128)S(1)} fusion(f32[8,1024,128,4]{2,1,3,0:T(8,128)} %get-tuple-element.357, f32[8,4,128]{2,1,0:T(4,128)S(1)} %max.12, pred[128,1024]{0,1:T(8,128)(4,1)S(1)} %compare_and_fusion.2), kind=kLoop, calls=%fused_computation.10.clone.1 | loop fusion | flops 16773120 | bytes 16941056 | tf_op jit(solution)/shard_map/while/body/eval_jaxpr/reduce_sum | solution.py:79
  184.0 7.4 %fusion.92 = f32[8,4,128,64]{2,3,1,0:T(8,128)S(1)} fusion(bf16[1024,8,64,1]{0,2,3,1:T(8,128)(2,1)S(1)} %bitcast.103, f32[8,1024,128,4]{2,1,3,0:T(8,128)} %get-tuple-element.357, f32[8,4,128]{2,1,0:T(4,128)S(1)} %max.12, pred[128,1024]{0,1:T(8,128)(4,1)S(1)} %compare_and_fusion.2, f32[8,4,128,64]{2,3,1,0:T(8,128)S(1)} %get-tuple-element.378, ...), kind=kOutput, calls=%fused_computation.13.clone.1 | convolution fusion | flops 554434560 | bytes 20086784 | tf_op jit(solution)/shard_map/while/body/eval_jaxpr/kgqs,skd->kgqd/dot_general | solution.py:80
  200.7 9.1 %fusion.90 = f32[8,4,128]{2,1,0:T(4,128)S(1)} fusion(f32[8,1024,128,4]{2,1,3,0:T(8,128)} %get-tuple-element.357, f32[8,4,128]{2,1,0:T(4,128)S(1)} %max.12, pred[128,1024]{0,1:T(8,128)(4,1)S(1)} %compare_and_fusion.2), kind=kLoop, calls=%fused_computation.10.clone.1 | loop fusion | flops 16773120 | bytes 16941056 | tf_op jit(solution)/shard_map/while/body/eval_jaxpr/reduce_sum | solution.py:79
  209.8 7.4 %fusion.92 = f32[8,4,128,64]{2,3,1,0:T(8,128)S(1)} fusion(bf16[1024,8,64,1]{0,2,3,1:T(8,128)(2,1)S(1)} %bitcast.103, f32[8,1024,128,4]{2,1,3,0:T(8,128)} %get-tuple-element.357, f32[8,4,128]{2,1,0:T(4,128)S(1)} %max.12, pred[128,1024]{0,1:T(8,128)(4,1)S(1)} %compare_and_fusion.2, f32[8,4,128,64]{2,3,1,0:T(8,128)S(1)} %get-tuple-element.378, ...), kind=kOutput, calls=%fused_computation.13.clone.1 | convolution fusion | flops 554434560 | bytes 20086784 | tf_op jit(solution)/shard_map/while/body/eval_jaxpr/kgqs,skd->kgqd/dot_general | solution.py:80
  226.5 9.1 %fusion.90 = f32[8,4,128]{2,1,0:T(4,128)S(1)} fusion(f32[8,1024,128,4]{2,1,3,0:T(8,128)} %get-tuple-element.357, f32[8,4,128]{2,1,0:T(4,128)S(1)} %max.12, pred[128,1024]{0,1:T(8,128)(4,1)S(1)} %compare_and_fusion.2), kind=kLoop, calls=%fused_computation.10.clone.1 | loop fusion | flops 16773120 | bytes 16941056 | tf_op jit(solution)/shard_map/while/body/eval_jaxpr/reduce_sum | solution.py:79
  235.7 7.4 %fusion.92 = f32[8,4,128,64]{2,3,1,0:T(8,128)S(1)} fusion(bf16[1024,8,64,1]{0,2,3,1:T(8,128)(2,1)S(1)} %bitcast.103, f32[8,1024,128,4]{2,1,3,0:T(8,128)} %get-tuple-element.357, f32[8,4,128]{2,1,0:T(4,128)S(1)} %max.12, pred[128,1024]{0,1:T(8,128)(4,1)S(1)} %compare_and_fusion.2, f32[8,4,128,64]{2,3,1,0:T(8,128)S(1)} %get-tuple-element.378, ...), kind=kOutput, calls=%fused_computation.13.clone.1 | convolution fusion | flops 554434560 | bytes 20086784 | tf_op jit(solution)/shard_map/while/body/eval_jaxpr/kgqs,skd->kgqd/dot_general | solution.py:80
  252.3 9.1 %fusion.90 = f32[8,4,128]{2,1,0:T(4,128)S(1)} fusion(f32[8,1024,128,4]{2,1,3,0:T(8,128)} %get-tuple-element.357, f32[8,4,128]{2,1,0:T(4,128)S(1)} %max.12, pred[128,1024]{0,1:T(8,128)(4,1)S(1)} %compare_and_fusion.2), kind=kLoop, calls=%fused_computation.10.clone.1 | loop fusion | flops 16773120 | bytes 16941056 | tf_op jit(solution)/shard_map/while/body/eval_jaxpr/reduce_sum | solution.py:79
  261.5 7.4 %fusion.92 = f32[8,4,128,64]{2,3,1,0:T(8,128)S(1)} fusion(bf16[1024,8,64,1]{0,2,3,1:T(8,128)(2,1)S(1)} %bitcast.103, f32[8,1024,128,4]{2,1,3,0:T(8,128)} %get-tuple-element.357, f32[8,4,128]{2,1,0:T(4,128)S(1)} %max.12, pred[128,1024]{0,1:T(8,128)(4,1)S(1)} %compare_and_fusion.2, f32[8,4,128,64]{2,3,1,0:T(8,128)S(1)} %get-tuple-element.378, ...), kind=kOutput, calls=%fused_computation.13.clone.1 | convolution fusion | flops 554434560 | bytes 20086784 | tf_op jit(solution)/shard_map/while/body/eval_jaxpr/kgqs,skd->kgqd/dot_general | solution.py:80
  286.4 16.3 %scatter_custom_fusion = bf16[640,2880]{1,0:T(8,128)(2,1)} fusion(s32[512]{0:T(512)S(1)} %bitcast.113, bf16[128,2880]{1,0:T(8,128)(2,1)S(1)} %copy.59, s32[1024]{0:T(1024)S(1)} %pad_clamp_fusion.1, bf16[]{:T(256)} %constant.192.clone.1), kind=kCustom, calls=%fused_computation.45 | custom fusion | bytes 3686402 | tf_op jit(solution)/shard_map/scatter | solution.py:151
  302.7 7.4 %reshape_reshape.3 = bf16[128,5,2880]{2,1,0:T(8,128)(2,1)} reshape(bf16[640,2880]{1,0:T(8,128)(2,1)} %scatter_custom_fusion) | data formatting | bytes 7372800 | tf_op jit(solution)/shard_map/reshape;reshape | solution.py:158
  310.1 80.1 %all_to_all.10 = bf16[128,5,2880]{2,1,0:T(8,128)(2,1)} all-to-all(bf16[128,5,2880]{2,1,0:T(8,128)(2,1)} %reshape_reshape.3), channel_id=1, replica_groups=mesh['ctx'=16,'grp'=8] {'ctx','grp'}, dimensions={0} | all-to-all | bytes 7372800 | tf_op jit(solution)/shard_map/all_to_all | solution.py:159
  390.2 7.9 %copy.60 = bf16[128,5,2880]{0,2,1:T(8,128)(2,1)} copy(bf16[128,5,2880]{2,1,0:T(8,128)(2,1)} %all_to_all.10) | data formatting | bytes 7372800 | tf_op jit(solution)/shard_map/all_to_all | solution.py:159
  405.7 8.5 %copy.61 = bf16[128,5,2880]{2,1,0:T(8,128)(2,1)} copy(bf16[128,5,2880]{0,2,1:T(8,128)(2,1)} %collective-permute-done.2) | data formatting | bytes 7372800 | tf_op jit(solution)/shard_map/ppermute | solution.py:160
  414.2 8.0 %reshape.328 = bf16[640,2880]{1,0:T(8,128)(2,1)} reshape(bf16[128,5,2880]{2,1,0:T(8,128)(2,1)} %copy.61) | data formatting | bytes 7372800 | tf_op jit(solution)/shard_map/reshape | solution.py:163
  422.3 9.9 %fusion.22 = f32[640,1536]{1,0:T(8,128)S(1)} fusion(bf16[640,2880]{1,0:T(8,128)(2,1)} %reshape.328, bf16[1,2880,1536]{2,1,0:T(8,128)(2,1)} %param.24), kind=kOutput, calls=%fused_computation.35 | convolution fusion | flops 5662310400 | bytes 16465920 | tf_op jit(solution)/shard_map/dot_general | solution.py:163
  432.1 7.9 %convolution_convert_fusion = bf16[640,2880]{0,1:T(8,128)(2,1)} fusion(bf16[1,768,2880]{1,2,0:T(8,128)(2,1)} %param.25, f32[640,1536]{1,0:T(8,128)S(1)} %fusion.22), kind=kOutput, calls=%fused_computation.41 | convolution fusion | flops 2836930560 | bytes 12042240 | tf_op jit(solution)/shard_map/dot_general | solution.py:165
  440.4 8.4 %reshape.327 = bf16[640,2880]{1,0:T(8,128)(2,1)} reshape(bf16[128,5,2880]{2,1,0:T(8,128)(2,1)} %all_to_all.10) | data formatting | bytes 7372800 | tf_op jit(solution)/shard_map/reshape | solution.py:163
  448.8 9.9 %fusion.24 = f32[640,1536]{1,0:T(8,128)S(1)} fusion(bf16[640,2880]{1,0:T(8,128)(2,1)} %reshape.327, bf16[1,2880,1536]{2,1,0:T(8,128)(2,1)} %param.24), kind=kOutput, calls=%fused_computation.37 | convolution fusion | flops 5662310400 | bytes 16465920 | tf_op jit(solution)/shard_map/dot_general | solution.py:163
  458.6 9.0 %add_convert_fusion = bf16[640,2880]{0,1:T(8,128)(2,1)} fusion(bf16[640,2880]{0,1:T(8,128)(2,1)} %collective-permute-done.3, bf16[1,768,2880]{1,2,0:T(8,128)(2,1)} %param.25, f32[640,1536]{1,0:T(8,128)S(1)} %fusion.24), kind=kOutput, calls=%fused_computation.39 | convolution fusion | flops 2844303360 | bytes 15728640 | tf_op jit(solution)/shard_map/dot_general | solution.py:165
  473.8 7.4 %reshape.329 = bf16[128,5,2880]{2,1,0:T(8,128)(2,1)} reshape(bf16[640,2880]{1,0:T(8,128)(2,1)} %copy.62) | data formatting | bytes 7372800 | tf_op jit(solution)/shard_map/reshape | solution.py:172
  486.8 73.2 %all-to-all-done.1 = bf16[128,5,2880]{2,1,0:T(8,128)(2,1)} async-done(((bf16[128,5,2880]{2,1,0:T(8,128)(2,1)}), bf16[128,5,2880]{2,1,0:T(8,128)(2,1)}, u32[]{:S(2)}, u32[]{:S(2)}) %all-to-all-start.1) | async-done | bytes 3686432 | tf_op jit(solution)/shard_map/all_to_all | solution.py:171
  560.0 8.0 %reshape.330 = bf16[640,2880]{1,0:T(8,128)(2,1)} reshape(bf16[128,5,2880]{2,1,0:T(8,128)(2,1)} %all-to-all-done.1) | data formatting | bytes 7372800 | tf_op jit(solution)/shard_map/reshape | solution.py:178
  568.0 9.3 %gather_fusion = bf16[512,2880]{1,0:T(8,128)(2,1)} fusion(bf16[640,2880]{1,0:T(8,128)(2,1)} %reshape.330, s32[1024]{0:T(1024)S(1)} %pad_clamp_fusion), kind=kCustom, calls=%fused_computation.1 | custom fusion | bytes 5900288 | tf_op jit(solution)/shard_map/gather | solution.py:179
  (134 shorter events, 94.9 us)
Async XLA Ops:
  7.2 3.6 copy-start
  7.2 4.9 copy-start.9
  7.2 5.3 copy-start.8
  7.2 5.4 copy-start.4
  7.2 105.5 %all-gather.3.cloned.1.call-start = ((), (), s32[]{:S(2)}) async-start(), calls=%async_computation.2 | async-start | bytes 13369344 | tf_op jit(solution)/shard_map/all_gather | solution.py:91
  10.7 260.0 %all-gather.5.cloned.1.call-start = ((), (), s32[]{:S(2)}) async-start(), calls=%async_computation.3 | async-start | bytes 6406144 | tf_op jit(solution)/shard_map/all_gather | solution.py:114
  269.2 2.7 collective-permute-start
  271.9 8.6 %copy-start.6 = (s32[1,128,4]{1,2,0:T(4,128)S(1)}, s32[1,128,4]{1,2,0:T(4,128)}, u32[]{:S(2)}) copy-start(s32[1,128,4]{1,2,0:T(4,128)} %param.23) | copy-start | bytes 6148
  277.2 1.6 copy-start.3
  278.7 6.8 %copy-start.7 = (f32[2880]{0:T(1024)S(1)}, f32[2880]{0:T(1024)}, u32[]{:S(2)}) copy-start(f32[2880]{0:T(1024)} %param.21) | copy-start | bytes 34564
  280.0 3.6 collective-permute-start.1
  285.6 306.9 %copy-start.2 = (bf16[128,2880]{0,1:T(8,128)(2,1)}, bf16[128,2880]{0,1:T(8,128)(2,1)S(1)}, u32[]{:S(2)}) copy-start(bf16[128,2880]{0,1:T(8,128)(2,1)S(1)} %get-tuple-element.287) | copy-start | bytes 2211844
  398.1 7.7 %collective-permute-start.2 = (bf16[128,5,2880]{0,2,1:T(8,128)(2,1)}, bf16[128,5,2880]{0,2,1:T(8,128)(2,1)}, u32[]{:S(2)}, u32[]{:S(2)}) collective-permute-start(bf16[128,5,2880]{0,2,1:T(8,128)(2,1)} %copy.60), channel_id=1, source_target_pairs={{0,1},{1,0},{2,3},{3,2},{4,5},{5,4},{6,7},{7,6},{8,9},{9,8},{10,11... | collective-permute-start | bytes 11059208 | tf_op jit(solution)/shard_map/ppermute | solution.py:160
  440.0 18.7 %collective-permute-start.3 = (bf16[640,2880]{0,1:T(8,128)(2,1)}, bf16[640,2880]{0,1:T(8,128)(2,1)}, u32[]{:S(2)}, u32[]{:S(2)}) collective-permute-start(bf16[640,2880]{0,1:T(8,128)(2,1)} %convolution_convert_fusion), channel_id=1, source_target_pairs={{0,1},{1,0},{2,3},{3,2},{4,5},{5,4},{6,7},{7,6},{8,9},{9,8},{10,11... | collective-permute-start | bytes 11059208 | tf_op jit(solution)/shard_map/ppermute | solution.py:169
  481.1 5.2 copy-start.5
  481.1 78.9 %all-to-all-start.1 = ((bf16[128,5,2880]{2,1,0:T(8,128)(2,1)}), bf16[128,5,2880]{2,1,0:T(8,128)(2,1)}, u32[]{:S(2)}, u32[]{:S(2)}) async-start(bf16[128,5,2880]{2,1,0:T(8,128)(2,1)} %reshape.329), calls=%async_computation.1 | async-start | bytes 12058624 | tf_op jit(solution)/shard_map/all_to_all | solution.py:171
  583.8 11.0 %copy-start.1 = (bf16[128,2880]{0,1:T(8,128)(2,1)S(1)}, bf16[128,2880]{0,1:T(8,128)(2,1)}, u32[]{:S(2)}) copy-start(bf16[128,2880]{0,1:T(8,128)(2,1)} %param.20) | copy-start | bytes 2211844
Sparse Core Ops, SparseCore 0:
  10.8 101.8 all-gather.2
  115.4 60.2 all-gather.4
where the time goes:
time: 612 us; the launch traced here: 602 us
  waiting for transfers between devices  181 us (30%)
  matrix products  130 us (21%)
  local copies, waits for them, and re-layouts  114 us (19%)
  blocking collectives  80.1 us (13%)
  other arithmetic  72.8 us (12%)
  between operations  14.5 us (2%)
  starting transfers between devices  8.92 us (1%)
    all_gather x1, waiting for transfers between devices, body(): piece = lax.all_gather(local_kv, 'ctx', axis=0, tiled=True)  99.8 us
    all_to_all x1, blocking collectives, body(): lax.all_to_all(split, ('ctx', 'grp'), split_axis=0, concat_axis=0, tiled=...  80.1 us
    all_to_all x1, waiting for transfers between devices, body(): lax.all_to_all(summed.reshape(owners, half_cap, width), ('ctx', 'grp'), s...  73.2 us
    reduce_sum x6, other arithmetic, key_block(): total = total * shrink + jnp.sum(weights, axis=-1)  54.9 us
    dot_general x6, matrix products, key_block(): jnp.einsum('kgqs,skd->kgqd', weights.astype(jnp.bfloat16), values, prefer...  44.9 us
    dot_general x6, matrix products, key_block(): jnp.einsum('qkgd,skd->kgqs', query_heads, keys, preferred_element_type=jn...  42.6 us
    dot_general x2, matrix products, expert_half(): jnp.dot(rows.reshape(-1, width), in_weights, preferred_element_type=jnp.f...  19.7 us
    dot_general x2, matrix products, expert_half(): jnp.dot(hidden, out_weights, preferred_element_type=jnp.float32)  16.8 us
  transfers between devices with their start and end apart: 7, of which 5 were waited for; matrix products, arithmetic and copies ran while one was open for 30% of the time, Pallas kernels for 0%

commit v1 on v0

--- a/solution.py
+++ b/solution.py
@@ -7,6 +7,15 @@
 HEADS = 32
 KVH = 8
 HD = 64
+
+
+def direct_the_masks(w_in, along_dim):
+    vals = []
+    for _ in range(jax.lax.axis_size("ctx")):
+        vals.append(w_in)
+    now = jax.lax.all_to_all(jnp.stack(vals, 0), "ctx", 0, 0)
+    w1 = jnp.concatenate(now, axis=along_dim)
+    return w1
 
 
 def doc_index(positions, lengths):
@@ -88,7 +97,7 @@
     start_top = jnp.broadcast_to(sink_grid[:, :, None], (KVH, groups, tokens))
     start_total = jnp.zeros((KVH, groups, tokens), jnp.float32)
     start_numer = jnp.zeros((KVH, groups, tokens, HD), jnp.float32)
-    piece = lax.all_gather(local_kv, "ctx", axis=0, tiled=True)
+    piece = direct_the_masks(local_kv, 0)
     count = piece.shape[0]
     step_rows = math.gcd(count, 1024)
 

time: 612 us -> 779 us (1.27)
  waiting for transfers between devices: 181 us -> 295 us
  local copies, waits for them, and re-layouts: 114 us -> 152 us
  starting transfers between devices: 8.92 us -> 17 us
    all_to_all x0 -> x1, waiting for transfers between devices: none -> 214 us  [direct_the_masks(): now = jax.lax.all_to_all(jnp.stack(vals, 0), 'ctx', 0, 0)]
    all_gather x1 -> x0, waiting for transfers between devices: 99.8 us -> none  [body(): piece = lax.all_gather(local_kv, 'ctx', axis=0, tiled=True)]
    all_to_all x0 -> x1, local copies, waits for them, and re-layouts: none -> 16.6 us  [direct_the_masks(): now = jax.lax.all_to_all(jnp.stack(vals, 0), 'ctx', 0, 0)]
    while x6 -> x18, local copies, waits for them, and re-layouts: 0.02 us -> 12.1 us
  transfers between devices with their start and end apart: 7 -> 7, of which waited for: 5 -> 5; matrix products, arithmetic and copies ran while one was open for 30% -> 29% of each run, Pallas kernels for 0% -> 0%
where the time goes in v1:
time: 779 us; the launch traced here: 768 us
  waiting for transfers between devices  295 us (38%)
  local copies, waits for them, and re-layouts  152 us (20%)
  matrix products  136 us (17%)
  blocking collectives  78.7 us (10%)
  other arithmetic  73.9 us (9%)
  starting transfers between devices  17 us (2%)
  between operations  14.5 us (2%)
    all_to_all x1, waiting for transfers between devices, direct_the_masks(): now = jax.lax.all_to_all(jnp.stack(vals, 0), 'ctx', 0, 0)  214 us
    all_to_all x1, blocking collectives, body(): lax.all_to_all(split, ('ctx', 'grp'), split_axis=0, concat_axis=0, tiled=...  78.7 us
    all_to_all x1, waiting for transfers between devices, body(): lax.all_to_all(summed.reshape(owners, half_cap, width), ('ctx', 'grp'), s...  73.2 us
    reduce_sum x6, other arithmetic, key_block(): total = total * shrink + jnp.sum(weights, axis=-1)  54.5 us
    dot_general x6, matrix products, key_block(): jnp.einsum('kgqs,skd->kgqd', weights.astype(jnp.bfloat16), values, prefer...  51.9 us
    dot_general x6, matrix products, key_block(): jnp.einsum('qkgd,skd->kgqs', query_heads, keys, preferred_element_type=jn...  42.3 us
    dot_general x2, matrix products, expert_half(): jnp.dot(rows.reshape(-1, width), in_weights, preferred_element_type=jnp.f...  19.7 us
    dot_general x2, matrix products, expert_half(): jnp.dot(hidden, out_weights, preferred_element_type=jnp.float32)  16.8 us
  transfers between devices with their start and end apart: 7, of which 5 were waited for; matrix products, arithmetic and copies ran while one was open for 29% of the time, Pallas kernels for 0%

profile of v1, /device:TPU:1, one launch (start us, length us, event | category | flops | bytes accessed | tf_op | source)
XLA Modules:
  0.0 768.4 jit_solution(3767584308005152845)
XLA Ops:
  14.9 7.8 %all-to-all-start = ((bf16[16,384,1024]{1,2,0:T(8,128)(2,1)}), bf16[16,384,1024]{1,2,0:T(8,128)(2,1)}, u32[]{:S(2)}, u32[]{:S(2)}) async-start(bf16[16,384,1024]{1,2,0:T(8,128)(2,1)} %stack.2), calls=%async_computation | async-start | bytes 25165824 | tf_op jit(solution)/shard_map/all_to_all | solution.py:16
  24.9 213.6 %all-to-all-done = bf16[16,384,1024]{1,2,0:T(8,128)(2,1)} async-done(((bf16[16,384,1024]{1,2,0:T(8,128)(2,1)}), bf16[16,384,1024]{1,2,0:T(8,128)(2,1)}, u32[]{:S(2)}, u32[]{:S(2)}) %all-to-all-start) | async-done | bytes 12582944 | tf_op jit(solution)/shard_map/all_to_all | solution.py:16
  238.5 16.6 %copy.66 = bf16[16,384,1024]{2,1,0:T(8,128)(2,1)} copy(bf16[16,384,1024]{1,2,0:T(8,128)(2,1)} %all-to-all-done) | data formatting | bytes 25165824 | tf_op jit(solution)/shard_map/all_to_all | solution.py:16
  255.2 180.0 %while.20 = (s32[]{:T(128)}, f32[8,4,128]{2,1,0:T(4,128)S(1)}, f32[8,4,128]{2,1,0:T(4,128)S(1)}, f32[8,4,128,64]{2,3,1,0:T(8,128)}, s32[1,8]{1,0:T(1,128)S(1)}, ...) while((s32[]{:T(128)}, f32[8,4,128]{2,1,0:T(4,128)S(1)}, ...), condition=%wide.region_7.8_spmd.clone, body=%wide.region_3.7_spmd.clone.sunk | while | flops 1121116288 | bytes 64247544 | solution.py:109
  266.9 9.1 %fusion.90 = f32[8,4,128]{2,1,0:T(4,128)S(1)} fusion(f32[8,1024,128,4]{2,1,3,0:T(8,128)} %get-tuple-element.375, f32[8,4,128]{2,1,0:T(4,128)S(1)} %max.12, pred[128,1024]{0,1:T(8,128)(4,1)S(1)} %compare_and_fusion.2), kind=kLoop, calls=%fused_computation.10.clone.1 | loop fusion | flops 16773120 | bytes 16941056 | tf_op jit(solution)/shard_map/while/body/eval_jaxpr/reduce_sum | solution.py:88
  276.5 8.4 %fusion.92 = f32[8,4,128,64]{2,3,1,0:T(8,128)} fusion(bf16[1024,8,64,1]{0,2,3,1:T(8,128)(2,1)S(1)} %bitcast.105, f32[8,1024,128,4]{2,1,3,0:T(8,128)} %get-tuple-element.375, f32[8,4,128]{2,1,0:T(4,128)S(1)} %max.12, pred[128,1024]{0,1:T(8,128)(4,1)S(1)} %compare_and_fusion.2, f32[8,4,128,64]{2,3,1,0:T(8,128)} %get-tuple-element.396, ...), kind=kOutput, calls=%fused_computation.13.clone.1 | convolution fusion | flops 554434560 | bytes 20086784 | tf_op jit(solution)/shard_map/while/body/eval_jaxpr/kgqs,skd->kgqd/dot_general | solution.py:89
  289.6 7.0 fusion.89
  296.6 9.1 %fusion.90 = f32[8,4,128]{2,1,0:T(4,128)S(1)} fusion(f32[8,1024,128,4]{2,1,3,0:T(8,128)} %get-tuple-element.375, f32[8,4,128]{2,1,0:T(4,128)S(1)} %max.12, pred[128,1024]{0,1:T(8,128)(4,1)S(1)} %compare_and_fusion.2), kind=kLoop, calls=%fused_computation.10.clone.1 | loop fusion | flops 16773120 | bytes 16941056 | tf_op jit(solution)/shard_map/while/body/eval_jaxpr/reduce_sum | solution.py:88
  306.3 8.7 %fusion.92 = f32[8,4,128,64]{2,3,1,0:T(8,128)} fusion(bf16[1024,8,64,1]{0,2,3,1:T(8,128)(2,1)S(1)} %bitcast.105, f32[8,1024,128,4]{2,1,3,0:T(8,128)} %get-tuple-element.375, f32[8,4,128]{2,1,0:T(4,128)S(1)} %max.12, pred[128,1024]{0,1:T(8,128)(4,1)S(1)} %compare_and_fusion.2, f32[8,4,128,64]{2,3,1,0:T(8,128)} %get-tuple-element.396, ...), kind=kOutput, calls=%fused_computation.13.clone.1 | convolution fusion | flops 554434560 | bytes 20086784 | tf_op jit(solution)/shard_map/while/body/eval_jaxpr/kgqs,skd->kgqd/dot_general | solution.py:89
  326.7 9.1 %fusion.90 = f32[8,4,128]{2,1,0:T(4,128)S(1)} fusion(f32[8,1024,128,4]{2,1,3,0:T(8,128)} %get-tuple-element.375, f32[8,4,128]{2,1,0:T(4,128)S(1)} %max.12, pred[128,1024]{0,1:T(8,128)(4,1)S(1)} %compare_and_fusion.2), kind=kLoop, calls=%fused_computation.10.clone.1 | loop fusion | flops 16773120 | bytes 16941056 | tf_op jit(solution)/shard_map/while/body/eval_jaxpr/reduce_sum | solution.py:88
  336.3 8.7 %fusion.92 = f32[8,4,128,64]{2,3,1,0:T(8,128)} fusion(bf16[1024,8,64,1]{0,2,3,1:T(8,128)(2,1)S(1)} %bitcast.105, f32[8,1024,128,4]{2,1,3,0:T(8,128)} %get-tuple-element.375, f32[8,4,128]{2,1,0:T(4,128)S(1)} %max.12, pred[128,1024]{0,1:T(8,128)(4,1)S(1)} %compare_and_fusion.2, f32[8,4,128,64]{2,3,1,0:T(8,128)} %get-tuple-element.396, ...), kind=kOutput, calls=%fused_computation.13.clone.1 | convolution fusion | flops 554434560 | bytes 20086784 | tf_op jit(solution)/shard_map/while/body/eval_jaxpr/kgqs,skd->kgqd/dot_general | solution.py:89
  356.7 9.1 %fusion.90 = f32[8,4,128]{2,1,0:T(4,128)S(1)} fusion(f32[8,1024,128,4]{2,1,3,0:T(8,128)} %get-tuple-element.375, f32[8,4,128]{2,1,0:T(4,128)S(1)} %max.12, pred[128,1024]{0,1:T(8,128)(4,1)S(1)} %compare_and_fusion.2), kind=kLoop, calls=%fused_computation.10.clone.1 | loop fusion | flops 16773120 | bytes 16941056 | tf_op jit(solution)/shard_map/while/body/eval_jaxpr/reduce_sum | solution.py:88
  366.4 8.7 %fusion.92 = f32[8,4,128,64]{2,3,1,0:T(8,128)} fusion(bf16[1024,8,64,1]{0,2,3,1:T(8,128)(2,1)S(1)} %bitcast.105, f32[8,1024,128,4]{2,1,3,0:T(8,128)} %get-tuple-element.375, f32[8,4,128]{2,1,0:T(4,128)S(1)} %max.12, pred[128,1024]{0,1:T(8,128)(4,1)S(1)} %compare_and_fusion.2, f32[8,4,128,64]{2,3,1,0:T(8,128)} %get-tuple-element.396, ...), kind=kOutput, calls=%fused_computation.13.clone.1 | convolution fusion | flops 554434560 | bytes 20086784 | tf_op jit(solution)/shard_map/while/body/eval_jaxpr/kgqs,skd->kgqd/dot_general | solution.py:89
  386.8 9.1 %fusion.90 = f32[8,4,128]{2,1,0:T(4,128)S(1)} fusion(f32[8,1024,128,4]{2,1,3,0:T(8,128)} %get-tuple-element.375, f32[8,4,128]{2,1,0:T(4,128)S(1)} %max.12, pred[128,1024]{0,1:T(8,128)(4,1)S(1)} %compare_and_fusion.2), kind=kLoop, calls=%fused_computation.10.clone.1 | loop fusion | flops 16773120 | bytes 16941056 | tf_op jit(solution)/shard_map/while/body/eval_jaxpr/reduce_sum | solution.py:88
  396.4 8.7 %fusion.92 = f32[8,4,128,64]{2,3,1,0:T(8,128)} fusion(bf16[1024,8,64,1]{0,2,3,1:T(8,128)(2,1)S(1)} %bitcast.105, f32[8,1024,128,4]{2,1,3,0:T(8,128)} %get-tuple-element.375, f32[8,4,128]{2,1,0:T(4,128)S(1)} %max.12, pred[128,1024]{0,1:T(8,128)(4,1)S(1)} %compare_and_fusion.2, f32[8,4,128,64]{2,3,1,0:T(8,128)} %get-tuple-element.396, ...), kind=kOutput, calls=%fused_computation.13.clone.1 | convolution fusion | flops 554434560 | bytes 20086784 | tf_op jit(solution)/shard_map/while/body/eval_jaxpr/kgqs,skd->kgqd/dot_general | solution.py:89
  416.8 9.1 %fusion.90 = f32[8,4,128]{2,1,0:T(4,128)S(1)} fusion(f32[8,1024,128,4]{2,1,3,0:T(8,128)} %get-tuple-element.375, f32[8,4,128]{2,1,0:T(4,128)S(1)} %max.12, pred[128,1024]{0,1:T(8,128)(4,1)S(1)} %compare_and_fusion.2), kind=kLoop, calls=%fused_computation.10.clone.1 | loop fusion | flops 16773120 | bytes 16941056 | tf_op jit(solution)/shard_map/while/body/eval_jaxpr/reduce_sum | solution.py:88
  426.5 8.7 %fusion.92 = f32[8,4,128,64]{2,3,1,0:T(8,128)} fusion(bf16[1024,8,64,1]{0,2,3,1:T(8,128)(2,1)S(1)} %bitcast.105, f32[8,1024,128,4]{2,1,3,0:T(8,128)} %get-tuple-element.375, f32[8,4,128]{2,1,0:T(4,128)S(1)} %max.12, pred[128,1024]{0,1:T(8,128)(4,1)S(1)} %compare_and_fusion.2, f32[8,4,128,64]{2,3,1,0:T(8,128)} %get-tuple-element.396, ...), kind=kOutput, calls=%fused_computation.13.clone.1 | convolution fusion | flops 554434560 | bytes 20086784 | tf_op jit(solution)/shard_map/while/body/eval_jaxpr/kgqs,skd->kgqd/dot_general | solution.py:89
  454.3 16.3 %scatter_custom_fusion = bf16[640,2880]{1,0:T(8,128)(2,1)} fusion(s32[512]{0:T(512)S(1)} %bitcast.115, bf16[128,2880]{1,0:T(8,128)(2,1)S(1)} %copy.74, s32[1024]{0:T(1024)S(1)} %pad_clamp_fusion.1, bf16[]{:T(256)} %constant.192.clone.1), kind=kCustom, calls=%fused_computation.45 | custom fusion | bytes 3686402 | tf_op jit(solution)/shard_map/scatter | solution.py:160
  470.6 7.4 reshape_reshape.3
  478.0 78.7 %all_to_all.15 = bf16[128,5,2880]{2,1,0:T(8,128)(2,1)} all-to-all(bf16[128,5,2880]{2,1,0:T(8,128)(2,1)} %reshape_reshape.3), channel_id=1, replica_groups=mesh['ctx'=16,'grp'=8] {'ctx','grp'}, dimensions={0} | all-to-all | bytes 7372800 | tf_op jit(solution)/shard_map/all_to_all | solution.py:168
  556.7 7.9 %copy.75 = bf16[128,5,2880]{0,2,1:T(8,128)(2,1)} copy(bf16[128,5,2880]{2,1,0:T(8,128)(2,1)} %all_to_all.15) | data formatting | bytes 7372800 | tf_op jit(solution)/shard_map/all_to_all | solution.py:168
  572.3 8.5 %copy.76 = bf16[128,5,2880]{2,1,0:T(8,128)(2,1)} copy(bf16[128,5,2880]{0,2,1:T(8,128)(2,1)} %collective-permute-done.2) | data formatting | bytes 7372800 | tf_op jit(solution)/shard_map/ppermute | solution.py:169
  580.8 8.0 %reshape.334 = bf16[640,2880]{1,0:T(8,128)(2,1)} reshape(bf16[128,5,2880]{2,1,0:T(8,128)(2,1)} %copy.76) | data formatting | bytes 7372800 | tf_op jit(solution)/shard_map/reshape | solution.py:172
  588.8 9.9 %fusion.22 = f32[640,1536]{1,0:T(8,128)S(1)} fusion(bf16[640,2880]{1,0:T(8,128)(2,1)} %reshape.334, bf16[1,2880,1536]{2,1,0:T(8,128)(2,1)} %param.24), kind=kOutput, calls=%fused_computation.35 | convolution fusion | flops 5662310400 | bytes 16465920 | tf_op jit(solution)/shard_map/dot_general | solution.py:172
  598.7 7.9 %convolution_convert_fusion = bf16[640,2880]{0,1:T(8,128)(2,1)} fusion(bf16[1,768,2880]{1,2,0:T(8,128)(2,1)} %param.25, f32[640,1536]{1,0:T(8,128)S(1)} %fusion.22), kind=kOutput, calls=%fused_computation.41 | convolution fusion | flops 2836930560 | bytes 12042240 | tf_op jit(solution)/shard_map/dot_general | solution.py:174
  606.9 8.4 %reshape.333 = bf16[640,2880]{1,0:T(8,128)(2,1)} reshape(bf16[128,5,2880]{2,1,0:T(8,128)(2,1)} %all_to_all.15) | data formatting | bytes 7372800 | tf_op jit(solution)/shard_map/reshape | solution.py:172
  615.3 9.9 %fusion.24 = f32[640,1536]{1,0:T(8,128)S(1)} fusion(bf16[640,2880]{1,0:T(8,128)(2,1)} %reshape.333, bf16[1,2880,1536]{2,1,0:T(8,128)(2,1)} %param.24), kind=kOutput, calls=%fused_computation.37 | convolution fusion | flops 5662310400 | bytes 16465920 | tf_op jit(solution)/shard_map/dot_general | solution.py:172
  625.2 9.0 %add_convert_fusion = bf16[640,2880]{0,1:T(8,128)(2,1)} fusion(bf16[640,2880]{0,1:T(8,128)(2,1)} %collective-permute-done.3, bf16[1,768,2880]{1,2,0:T(8,128)(2,1)} %param.25, f32[640,1536]{1,0:T(8,128)S(1)} %fusion.24), kind=kOutput, calls=%fused_computation.39 | convolution fusion | flops 2844303360 | bytes 15728640 | tf_op jit(solution)/shard_map/dot_general | solution.py:174
  640.3 7.4 reshape.335
  653.3 73.2 %all-to-all-done.2 = bf16[128,5,2880]{2,1,0:T(8,128)(2,1)} async-done(((bf16[128,5,2880]{2,1,0:T(8,128)(2,1)}), bf16[128,5,2880]{2,1,0:T(8,128)(2,1)}, u32[]{:S(2)}, u32[]{:S(2)}) %all-to-all-start.2) | async-done | bytes 3686432 | tf_op jit(solution)/shard_map/all_to_all | solution.py:180
  726.5 8.0 %reshape.336 = bf16[640,2880]{1,0:T(8,128)(2,1)} reshape(bf16[128,5,2880]{2,1,0:T(8,128)(2,1)} %all-to-all-done.2) | data formatting | bytes 7372800 | tf_op jit(solution)/shard_map/reshape | solution.py:187
  734.5 9.3 %gather_fusion = bf16[512,2880]{1,0:T(8,128)(2,1)} fusion(bf16[640,2880]{1,0:T(8,128)(2,1)} %reshape.336, s32[1024]{0:T(1024)S(1)} %pad_clamp_fusion), kind=kCustom, calls=%fused_computation.1 | custom fusion | bytes 5900288 | tf_op jit(solution)/shard_map/gather | solution.py:188
  (146 shorter events, 132.5 us)
Async XLA Ops:
  7.2 15.6 %copy-start = (bf16[128,2880]{0,1:T(8,128)(2,1)S(1)}, bf16[128,2880]{0,1:T(8,128)(2,1)}, u32[]{:S(2)}) copy-start(bf16[128,2880]{0,1:T(8,128)(2,1)} %param.20) | copy-start | bytes 2211844
  14.9 9.2 %copy-start.9 = (s32[1,8]{1,0:T(1,128)S(1)}, s32[1,8]{1,0:T(1,128)}, u32[]{:S(2)}) copy-start(s32[1,8]{1,0:T(1,128)} %param.18) | copy-start | bytes 100
  14.9 9.6 %copy-start.8 = (f32[32]{0:T(128)S(1)}, f32[32]{0:T(128)}, u32[]{:S(2)}) copy-start(f32[32]{0:T(128)} %param.19) | copy-start | bytes 388
  14.9 9.6 %copy-start.4 = (bf16[1,128,2048]{2,1,0:T(8,128)(2,1)S(1)}, bf16[1,128,2048]{2,1,0:T(8,128)(2,1)}, u32[]{:S(2)}) copy-start(bf16[1,128,2048]{2,1,0:T(8,128)(2,1)} %param.15) | copy-start | bytes 1572868
  14.9 223.6 %all-to-all-start = ((bf16[16,384,1024]{1,2,0:T(8,128)(2,1)}), bf16[16,384,1024]{1,2,0:T(8,128)(2,1)}, u32[]{:S(2)}, u32[]{:S(2)}) async-start(bf16[16,384,1024]{1,2,0:T(8,128)(2,1)} %stack.2), calls=%async_computation | async-start | bytes 25165824 | tf_op jit(solution)/shard_map/all_to_all | solution.py:16
  22.7 416.1 %all-gather.2.cloned.1.call-start = ((), (), s32[]{:S(2)}) async-start(), calls=%async_computation.3 | async-start | bytes 6406144 | tf_op jit(solution)/shard_map/all_gather | solution.py:123
  436.7 3.2 collective-permute-start
  439.9 8.5 %copy-start.6 = (s32[1,128,4]{1,2,0:T(4,128)S(1)}, s32[1,128,4]{1,2,0:T(4,128)}, u32[]{:S(2)}) copy-start(s32[1,128,4]{1,2,0:T(4,128)} %param.23) | copy-start | bytes 6148
  445.2 1.6 copy-start.3
  446.8 6.7 copy-start.7
  448.0 3.5 collective-permute-start.1
  453.5 305.5 %copy-start.2 = (bf16[128,2880]{0,1:T(8,128)(2,1)}, bf16[128,2880]{0,1:T(8,128)(2,1)S(1)}, u32[]{:S(2)}) copy-start(bf16[128,2880]{0,1:T(8,128)(2,1)S(1)} %get-tuple-element.305) | copy-start | bytes 2211844
  564.6 7.7 collective-permute-start.2
  606.5 18.6 %collective-permute-start.3 = (bf16[640,2880]{0,1:T(8,128)(2,1)}, bf16[640,2880]{0,1:T(8,128)(2,1)}, u32[]{:S(2)}, u32[]{:S(2)}) collective-permute-start(bf16[640,2880]{0,1:T(8,128)(2,1)} %convolution_convert_fusion), channel_id=1, source_target_pairs={{0,1},{1,0},{2,3},{3,2},{4,5},{5,4},{6,7},{7,6},{8,9},{9,8},{10,11... | collective-permute-start | bytes 11059208 | tf_op jit(solution)/shard_map/ppermute | solution.py:178
  647.7 5.2 copy-start.5
  647.7 78.9 %all-to-all-start.2 = ((bf16[128,5,2880]{2,1,0:T(8,128)(2,1)}), bf16[128,5,2880]{2,1,0:T(8,128)(2,1)}, u32[]{:S(2)}, u32[]{:S(2)}) async-start(bf16[128,5,2880]{2,1,0:T(8,128)(2,1)} %reshape.335), calls=%async_computation.2 | async-start | bytes 12058624 | tf_op jit(solution)/shard_map/all_to_all | solution.py:180
  750.4 11.0 %copy-start.1 = (bf16[128,2880]{0,1:T(8,128)(2,1)S(1)}, bf16[128,2880]{0,1:T(8,128)(2,1)}, u32[]{:S(2)}) copy-start(bf16[128,2880]{0,1:T(8,128)(2,1)} %param.20) | copy-start | bytes 2211844
Sparse Core Ops, SparseCore 0:
  26.2 207.7 all-gather.1
